TPU v7x, 32 devices: a whole 2x2x4 slice. The times are simulated.
32 devices in a mesh: grp: 2 (over y), seq: 4 (over z), head: 4 (over x, core).
Axes of the slice: x: 2, y: 2, z: 4, core: 2. Of those that a mesh axis runs over, the one named last changes fastest.
Arguments:
- lin_query: bfloat16 [2560, 8192], P(('grp', 'seq'), 'head'), parts along dimension 0, may hold values from -6 to 6
- lin_key: bfloat16 [2560, 8192], P(('grp', 'seq'), 'head'), parts along dimension 0, may hold values from -6 to 6
- lin_value: bfloat16 [2560, 8192], P(('grp', 'seq'), 'head'), parts along dimension 0, may hold values from -6 to 6
- norm_gain: bfloat16 [8192], P('head'), may hold values from 0.25 to 1.75
- out_gate: bfloat16 [2560, 8192], P(('grp', 'seq'), 'head'), parts along dimension 0, may hold values from -6 to 6
- soft_query: bfloat16 [2560, 8192], P(('grp', 'seq'), 'head'), parts along dimension 0, may hold values from -24 to 24
- soft_key: bfloat16 [2560, 8192], P(('grp', 'seq'), 'head'), parts along dimension 0, may hold values from -24 to 24
- doc_id: int32 [2560], P(('grp', 'seq')), parts along dimension 0, may hold values from 0 to 7, never falling along the last dimension, each value on 1 to 640 neighbouring positions
Outputs:
- lin_out: bfloat16 [2560, 8192], P(('grp', 'seq'), 'head'), parts along dimension 0
- soft_out: bfloat16 [2560, 8192], P(('grp', 'seq'), 'head'), parts along dimension 0
There are 2 independent parts, one for each index of `grp`. A program takes and returns all parts, laid end to end along the dimension named above; an argument that names none is the same for every part. Nothing has to cross between parts.
Inputs may be any that keep to these rules, and one draw needn't show every extreme that they name: `doc_id`: never falls along the sequence; every document holds 1 to half of 1280 tokens, and one holds exactly half of 1280.
All inputs are finite; a program needn't handle non-finite values.
Results may differ from a plain program's by a relative error of at most 0.0095.
Values may be sent and summed in bfloat16 or wider, within the bound.
No kernel may reach another device: no remote copies, remote signals or barrier semaphores. Data moves between devices by JAX's collectives and lax.ppermute only.
A program may use at most 192 MiB of HBM per device.

v0:
```python
import math
import jax
import jax.numpy as jnp
from jax import lax
from jax.sharding import PartitionSpec as P

HD = 128
norm_eps = 1e-06


def per_device(lin_query, lin_key, lin_value, norm_gain, out_gate, soft_query, soft_key, doc_id):
    row_count = lin_query.shape[0]
    head_count = lin_query.shape[1] // HD
    my_index = lax.axis_index("seq")
    queries = lin_query.reshape(row_count, head_count, HD)
    key_rows = lin_key.reshape(row_count, head_count, HD)
    value_rows = lin_value.reshape(row_count, head_count, HD)
    first_doc = doc_id[0]
    last_doc = doc_id[-1]
    tail_keys = jnp.where((doc_id == last_doc)[:, None, None], key_rows, jnp.zeros_like(key_rows))
    local_state = jnp.einsum(
        "thd,the->hde", tail_keys, value_rows, preferred_element_type=jnp.float32
    )
    empty_state = jnp.zeros_like(local_state)
    states = lax.all_gather(
        local_state[None].astype(jnp.bfloat16), "seq", axis=0, tiled=True
    ).astype(jnp.float32)
    tags = lax.all_gather(last_doc[None], "seq", axis=0, tiled=True)
    sources = jnp.arange(tags.shape[0], dtype=jnp.int32)
    wanted = (tags == first_doc) & (sources < my_index)
    carried = empty_state + jnp.sum(
        jnp.where(wanted[:, None, None, None], states, jnp.zeros_like(states)), axis=0
    )
    positions = jnp.arange(row_count, dtype=jnp.int32)
    causal = positions[:, None] >= positions[None, :]
    keep_local = causal & (doc_id[:, None] == doc_id[None, :])
    scores = jnp.einsum("qhd,khd->hqk", queries, key_rows, preferred_element_type=jnp.float32)
    rounded = jnp.where(keep_local[None], scores, jnp.zeros_like(scores)).astype(jnp.bfloat16)
    block_term = jnp.einsum("hqk,khd->qhd", rounded, value_rows, preferred_element_type=jnp.float32)
    carried_term = jnp.einsum(
        "qhd,hde->qhe", queries.astype(jnp.float32), carried, precision=lax.Precision.HIGHEST
    )
    carried_term = jnp.where(
        (doc_id == first_doc)[:, None, None], carried_term, jnp.zeros_like(carried_term)
    )
    lin_raw = block_term + carried_term
    mean_square = jnp.mean(lin_raw * lin_raw, axis=-1, keepdims=True)
    gain_rows = norm_gain.astype(jnp.float32).reshape(head_count, HD)
    gate_rows = jax.nn.sigmoid(out_gate.astype(jnp.float32).reshape(row_count, head_count, HD))
    normed = lin_raw * lax.rsqrt(mean_square + norm_eps) * gain_rows * gate_rows
    lin_out = normed.astype(jnp.bfloat16).reshape(row_count, head_count * HD)
    query_soft = soft_query.reshape(row_count, head_count, HD)
    query_pos = my_index * row_count + positions
    score_scale = 1.0 / math.sqrt(HD)
    key_flat = lax.all_gather(soft_key, "seq", axis=0, tiled=True)
    row_max = jnp.full((head_count, row_count), -1e30, jnp.float32)
    piece_rows = key_flat.shape[0]
    key_part = key_flat.reshape(piece_rows, head_count, HD)
    value_part = lax.all_gather(lin_out, "seq", axis=0, tiled=True).reshape(
        piece_rows, head_count, HD
    )
    key_pos = jnp.arange(piece_rows, dtype=jnp.int32)
    logits = (
        jnp.einsum("qhd,khd->hqk", query_soft, key_part, preferred_element_type=jnp.float32)
        * score_scale
    )
    keep_mask = (
        (query_pos[:, None] >= key_pos[None, :])
        & (doc_id[:, None] == lax.all_gather(doc_id, "seq", axis=0, tiled=True)[None, :])
        & True
    )
    logits = jnp.where(keep_mask[None], logits, -1e30)
    new_max = jnp.maximum(row_max, jnp.max(logits, axis=-1))
    probs = jnp.where(keep_mask[None], jnp.exp(logits - new_max[..., None]), 0.0)
    denom_sum = jnp.sum(probs, axis=-1)
    update = jnp.einsum(
        "hqk,khd->qhd", probs.astype(jnp.bfloat16), value_part, preferred_element_type=jnp.float32
    )
    soft_out = update / jnp.transpose(denom_sum)[:, :, None]
    return (lin_out, soft_out.astype(jnp.bfloat16).reshape(row_count, head_count * HD))


def solution(mesh):
    return jax.shard_map(
        per_device,
        mesh=mesh,
        in_specs=(
            P(("grp", "seq"), "head"),
            P(("grp", "seq"), "head"),
            P(("grp", "seq"), "head"),
            P("head"),
            P(("grp", "seq"), "head"),
            P(("grp", "seq"), "head"),
            P(("grp", "seq"), "head"),
            P(("grp", "seq")),
        ),
        out_specs=(P(("grp", "seq"), "head"), P(("grp", "seq"), "head")),
        check_vma=False,
    )
```

profile of v0, /device:TPU:0, one launch (start us, length us, event | category | flops | bytes accessed | tf_op | source)
XLA Modules:
  0.0 291.2 jit_solution(3869232572104715279)
XLA Ops:
  7.2 0.0 copy-start
  7.2 0.0 all-gather.9.cloned.1.call-start
  7.2 1.3 dynamic-slice
  8.6 2.0 fusion.52
  10.6 2.0 broadcast_compare_fusion.1
  12.5 0.0 copy-start.4
  12.5 0.0 copy-start.5
  12.5 3.4 %fusion.34 = bf16[16,128,128]{2,1,0:T(8,128)(2,1)} fusion(pred[320]{0:T(512)(128)(4,1)S(1)} %get-tuple-element.5, bf16[320,2048]{1,0:T(8,128)(2,1)} %param.10, bf16[320,2048]{1,0:T(8,128)(2,1)} %param.9), kind=kOutput, calls=%fused_computation.39 | convolution fusion | flops 168689664 | bytes 3146048 | tf_op jit(solution)/shard_map/thd,the->hde/dot_general | solution.py:21
  15.9 0.0 copy-start.3
  15.9 0.0 all-gather.9.cloned.1.call-update
  16.0 0.0 all-gather.7.cloned.1.call-start
  16.0 0.7 all-gather.7.cloned.1.call-update
  16.7 0.0 all-gather.5.cloned.1.call-start
  17.4 0.0 copy-done.4
  17.4 0.3 dynamic-update-slice.1
  17.7 10.1 %all-reduce.2 = (s32[4]{0:T(128)S(1)}, s32[1280]{0:T(1024)S(1)}) all-reduce(s32[4]{0:T(128)S(1)} %get-tuple-element.7, s32[1280]{0:T(1024)S(1)} %dynamic-update-slice.1), channel_id=1, replica_groups=mesh['grp'=2,'seq'=4,'head'=4] {'seq'}, use_global_device_ids=true, to_apply=%add | all-reduce | flops 1284 | bytes 10272
  27.8 0.6 compare_and_fusion
  28.5 0.0 copy-done.5
  28.5 0.1 fusion.46
  28.6 36.1 %all-gather.9.cloned.1.call-done = bf16[64,128,128]{2,1,0:T(8,128)(2,1)} async-done(((bf16[16,128,128]{2,1,0:T(8,128)(2,1)}), bf16[64,128,128]{2,1,0:T(8,128)(2,1)}) %all-gather.9.cloned.1.call-update) | async-done | bytes 2097168 | tf_op jit(solution)/shard_map/all_gather | solution.py:25
  64.8 2.2 fusion.6
  67.0 0.0 copy-done.3
  67.0 2.7 fusion.29
  69.7 0.0 copy-start.2
  69.7 7.2 %multiply_reduce_fusion = (f32[320,16]{0,1:T(8,128)S(1)}, f32[320,16,128]{2,0,1:T(8,128)}) fusion(f32[16,128,320]{1,2,0:T(8,128)} %fusion.29, pred[320]{0:T(512)(128)(4,1)S(1)} %get-tuple-element.4, pred[320,320]{1,0:T(8,128)(4,1)S(1)} %fusion.46, bf16[320,2048]{1,0:T(8,128)(2,1)} %param.10, bf16[320,2048]{1,0:T(8,128)(2,1)} %param.9, ...), kind=kOutput, calls=%fused_computation.20 | convolution fusion | flops 844753920 | bytes 9298240 | tf_op jit(solution)/shard_map/hqk,khd->qhd/dot_general | solution.py:39
  76.9 0.0 copy-done.2
  76.9 3.2 %copy_bitcast_fusion.1 = bf16[320,2048]{1,0:T(8,128)(2,1)} fusion(f32[320,16,128]{2,0,1:T(8,128)} %get-tuple-element.10, f32[16,128]{1,0:T(8,128)S(1)} %bitcast_convert_fusion, f32[320,16]{0,1:T(8,128)S(1)} %add_rsqrt_fusion, bf16[320,2048]{1,0:T(8,128)(2,1)S(1)} %copy-done.2), kind=kLoop, calls=%fused_computation.26 | loop fusion | flops 5242880 | bytes 5271552 | tf_op jit(solution)/shard_map/reshape | solution.py:51
  80.1 0.0 all-gather.5.cloned.1.call-update
  80.2 0.4 fusion.16
  80.6 82.6 %all-gather.7.cloned.1.call-done = bf16[1280,2048]{1,0:T(8,128)(2,1)} async-done(((bf16[320,2048]{1,0:T(8,128)(2,1)}), bf16[1280,2048]{1,0:T(8,128)(2,1)}) %all-gather.7.cloned.1.call-update) | async-done | bytes 5242896 | tf_op jit(solution)/shard_map/all_gather | solution.py:55
  163.1 7.9 %copy.36 = bf16[1280,2048]{0,1:T(8,128)(2,1)} copy(bf16[1280,2048]{1,0:T(8,128)(2,1)} %all-gather.7.cloned.1.call-done) | data formatting | bytes 10485760 | tf_op jit(solution)/shard_map/all_gather | solution.py:55
  171.1 0.0 copy-done
  171.1 13.3 %fusion = (f32[16,320]{1,0:T(8,128)S(1)}, f32[16,320,1280]{2,1,0:T(8,128)}) fusion(pred[320,1280]{1,0:T(8,128)(4,1)S(1)} %fusion.16, bf16[1280,16,128]{0,2,1:T(8,128)(2,1)} %bitcast.105, bf16[320,2048]{1,0:T(8,128)(2,1)S(1)} %copy-done), kind=kOutput, calls=%fused_computation.2 | convolution fusion | flops 1697377280 | bytes 33198080 | tf_op jit(solution)/shard_map/qhd,khd->hqk/dot_general | solution.py:64
  184.4 13.9 %fusion.1 = f32[16,320]{1,0:T(8,128)S(1)} fusion(f32[16,320,1280]{2,1,0:T(8,128)} %get-tuple-element.12, f32[16,320]{1,0:T(8,128)S(1)} %broadcast_maximum_fusion, pred[320,1280]{1,0:T(8,128)(4,1)S(1)} %fusion.16), kind=kLoop, calls=%fused_computation.3 | loop fusion | flops 32762880 | bytes 26664960 | tf_op jit(solution)/shard_map/reduce_sum | solution.py:75
  198.3 63.4 %all-gather.5.cloned.1.call-done = bf16[1280,2048]{1,0:T(8,128)(2,1)} async-done(((bf16[320,2048]{1,0:T(8,128)(2,1)}), bf16[1280,2048]{1,0:T(8,128)(2,1)}) %all-gather.5.cloned.1.call-update) | async-done | bytes 5242896 | tf_op jit(solution)/shard_map/all_gather | solution.py:59
  261.8 7.9 %copy.35 = bf16[1280,2048]{0,1:T(8,128)(2,1)} copy(bf16[1280,2048]{1,0:T(8,128)(2,1)} %all-gather.5.cloned.1.call-done) | data formatting | bytes 10485760 | tf_op jit(solution)/shard_map/all_gather | solution.py:59
  269.7 0.0 copy-start.1
  269.7 13.5 %fusion.17 = bf16[16,40,8,128]{3,2,1,0:T(8,128)(2,1)S(1)} fusion(bf16[1280,16,128]{0,2,1:T(8,128)(2,1)} %bitcast.106, f32[16,320,1280]{2,1,0:T(8,128)} %get-tuple-element.12, f32[16,320]{1,0:T(8,128)S(1)} %broadcast_maximum_fusion, pred[320,1280]{1,0:T(8,128)(4,1)S(1)} %fusion.16, f32[320,16]{0,1:T(8,128)S(1)} %bitcast.109), kind=kOutput, calls=%fused_computation.23 | convolution fusion | flops 1711800320 | bytes 33218560 | tf_op jit(solution)/shard_map/hqk,khd->qhd/dot_general | solution.py:76
  283.2 1.4 copy.94
  284.6 0.0 copy-done.1
  (6 shorter events, 0.0 us)
Async XLA Ops:
  7.2 163.9 %copy-start = (bf16[320,2048]{1,0:T(8,128)(2,1)S(1)}, bf16[320,2048]{1,0:T(8,128)(2,1)}, u32[]{:S(2)}) copy-start(bf16[320,2048]{1,0:T(8,128)(2,1)} %param.13) | copy-start | bytes 3932164
  7.2 57.6 %all-gather.9.cloned.1.call-start = ((), (), s32[]{:S(2)}) async-start(), calls=%async_computation.2 | async-start | bytes 2621440 | tf_op jit(solution)/shard_map/all_gather | solution.py:25
  12.5 4.9 %copy-start.4 = (s32[320]{0:T(512)S(1)}, s32[320]{0:T(512)}, u32[]{:S(2)}) copy-start(s32[320]{0:T(512)} %param.15) | copy-start | bytes 3844
  12.5 15.9 %copy-start.5 = (bf16[2048]{0:T(1024)(128)(2,1)S(1)}, bf16[2048]{0:T(1024)(128)(2,1)}, u32[]{:S(2)}) copy-start(bf16[2048]{0:T(1024)(128)(2,1)} %param.11) | copy-start | bytes 12292
  15.9 51.1 %copy-start.3 = (bf16[320,2048]{1,0:T(8,128)(2,1)S(1)}, bf16[320,2048]{1,0:T(8,128)(2,1)}, u32[]{:S(2)}) copy-start(bf16[320,2048]{1,0:T(8,128)(2,1)} %param.8) | copy-start | bytes 3932164
  16.0 147.2 %all-gather.7.cloned.1.call-start = ((), (), s32[]{:S(2)}) async-start(), calls=%async_computation.1 | async-start | bytes 6553600 | tf_op jit(solution)/shard_map/all_gather | solution.py:55
  16.7 245.0 %all-gather.5.cloned.1.call-start = ((), (), s32[]{:S(2)}) async-start(), calls=%async_computation | async-start | bytes 6553600 | tf_op jit(solution)/shard_map/all_gather | solution.py:59
  69.7 7.2 %copy-start.2 = (bf16[320,2048]{1,0:T(8,128)(2,1)S(1)}, bf16[320,2048]{1,0:T(8,128)(2,1)}, u32[]{:S(2)}) copy-start(bf16[320,2048]{1,0:T(8,128)(2,1)} %param.12) | copy-start | bytes 3932164
  269.7 15.0 %copy-start.1 = (bf16[320,2048]{1,0:T(8,128)(2,1)S(1)}, bf16[320,2048]{1,0:T(8,128)(2,1)}, u32[]{:S(2)}) copy-start(bf16[320,2048]{1,0:T(8,128)(2,1)} %param.13) | copy-start | bytes 3932164
Sparse Core Ops, SparseCore 0:
  16.1 48.6 all-gather.8
  66.3 96.7 all-gather.6
  165.3 96.4 all-gather.4
where the time goes:
time: 292 us; the launch traced here: 291 us
  waiting for transfers between devices  183 us (63%)
  matrix products  40.1 us (14%)
  other arithmetic  22.5 us (8%)
  local copies, waits for them, and re-layouts  20.9 us (7%)
  between operations  14.5 us (5%)
  blocking collectives  10.1 us (3%)
    all_gather x1, waiting for transfers between devices, per_device(): key_flat = lax.all_gather(soft_key, 'seq', axis=0, tiled=True)  82.6 us
    all_gather x1, waiting for transfers between devices, per_device(): lax.all_gather(lin_out, 'seq', axis=0, tiled=True)  63.4 us
    all_gather x1, waiting for transfers between devices, per_device(): lax.all_gather(local_state[None].astype(jnp.bfloat16), 'seq', axis=0, til...  36.1 us
    reduce_sum x1, other arithmetic, per_device(): denom_sum = jnp.sum(probs, axis=-1)  13.9 us
    dot_general x1, matrix products, per_device(): jnp.einsum('hqk,khd->qhd', probs.astype(jnp.bfloat16), value_part, prefer...  13.5 us
    dot_general x1, matrix products, per_device(): jnp.einsum('qhd,khd->hqk', query_soft, key_part, preferred_element_type=j...  13.3 us
    unnamed x1, blocking collectives  10.1 us
    all_gather x1, local copies, waits for them, and re-layouts, per_device(): key_flat = lax.all_gather(soft_key, 'seq', axis=0, tiled=True)  7.92 us
  transfers between devices with their start and end apart: 3, of which 3 were waited for; matrix products, arithmetic and copies ran while one was open for 18% of the time, Pallas kernels for 0%

commit v1 on v0

--- a/solution.py
+++ b/solution.py
@@ -6,6 +6,28 @@
 
 HD = 128
 norm_eps = 1e-06
+
+
+def joined_along(pieces, dim):
+    dims = list(pieces.shape[1:])
+    dims[dim] *= pieces.shape[0]
+    return jnp.moveaxis(pieces, 0, dim).reshape(dims)
+
+
+def doubled(shard, axis):
+    peers = lax.axis_size(axis)
+    blocks = shard[None]
+    for level in range(peers.bit_length() - 1):
+        bit = 1 << level
+        other = lax.ppermute(blocks, axis, [(i, i ^ bit) for i in range(peers)])
+        both = jnp.stack([blocks, other])
+        upper = lax.axis_index(axis) >> level & 1
+        blocks = jnp.where(upper == 0, both, both[::-1]).reshape(-1, *shard.shape)
+    return blocks
+
+
+def doubled_up(x, axis, dim):
+    return joined_along(doubled(x, axis), dim)
 
 
 def per_device(lin_query, lin_key, lin_value, norm_gain, out_gate, soft_query, soft_key, doc_id):
@@ -56,9 +78,7 @@
     row_max = jnp.full((head_count, row_count), -1e30, jnp.float32)
     piece_rows = key_flat.shape[0]
     key_part = key_flat.reshape(piece_rows, head_count, HD)
-    value_part = lax.all_gather(lin_out, "seq", axis=0, tiled=True).reshape(
-        piece_rows, head_count, HD
-    )
+    value_part = doubled_up(lin_out, "seq", 0).reshape(piece_rows, head_count, HD)
     key_pos = jnp.arange(piece_rows, dtype=jnp.int32)
     logits = (
         jnp.einsum("qhd,khd->hqk", query_soft, key_part, preferred_element_type=jnp.float32)

time: 292 us -> 368 us (1.26)
  waiting for transfers between devices: 183 us -> 244 us
  other arithmetic: 22.5 us -> 31.4 us
  local copies, waits for them, and re-layouts: 20.9 us -> 26.8 us
    ppermute x0 -> x2, waiting for transfers between devices: none -> 208 us  [doubled(): other = lax.ppermute(blocks, axis, [(i, i ^ bit) for i in range(peers)])]
    all_gather x1, waiting for transfers between devices: 82.6 us -> 0.01 us  [per_device(): key_flat = lax.all_gather(soft_key, 'seq', axis=0, tiled=True)]
    all_gather x1 -> x0, waiting for transfers between devices: 63.4 us -> none  [per_device(): lax.all_gather(lin_out, 'seq', axis=0, tiled=True)]
    all_gather x1 -> x0, local copies, waits for them, and re-layouts: 7.92 us -> none  [per_device(): lax.all_gather(lin_out, 'seq', axis=0, tiled=True)]
    another operation x0 -> x3, other arithmetic: none -> 7.63 us  [doubled(): both = jnp.stack([blocks, other])]
    another operation x0 -> x2, local copies, waits for them, and re-layouts: none -> 6.47 us  [the longest x1 3.25 us: doubled(): blocks = shard[None]]
    unnamed x16 -> x17, local copies, waits for them, and re-layouts: 1.65 us -> 5.81 us
  transfers between devices with their start and end apart: 3 -> 4, of which waited for: 3 -> 3; matrix products, arithmetic and copies ran while one was open for 18% -> 11% of each run, Pallas kernels for 0% -> 0%
where the time goes in v1:
time: 368 us; the launch traced here: 367 us
  waiting for transfers between devices  244 us (66%)
  matrix products  39.2 us (11%)
  other arithmetic  31.4 us (9%)
  local copies, waits for them, and re-layouts  26.8 us (7%)
  between operations  14.8 us (4%)
  blocking collectives  10.1 us (3%)
    ppermute x2, waiting for transfers between devices, doubled(): other = lax.ppermute(blocks, axis, [(i, i ^ bit) for i in range(peers)])  208 us
    all_gather x1, waiting for transfers between devices, per_device(): lax.all_gather(local_state[None].astype(jnp.bfloat16), 'seq', axis=0, til...  36 us
    reduce_sum x1, other arithmetic, per_device(): denom_sum = jnp.sum(probs, axis=-1)  13.9 us
    dot_general x1, matrix products, per_device(): jnp.einsum('hqk,khd->qhd', probs.astype(jnp.bfloat16), value_part, prefer...  13.7 us
    dot_general x1, matrix products, per_device(): jnp.einsum('qhd,khd->hqk', query_soft, key_part, preferred_element_type=j...  12.9 us
    unnamed x1, blocking collectives  10.1 us
    all_gather x1, local copies, waits for them, and re-layouts, per_device(): key_flat = lax.all_gather(soft_key, 'seq', axis=0, tiled=True)  7.92 us
    another operation x3, other arithmetic, doubled(): both = jnp.stack([blocks, other])  7.63 us
  transfers between devices with their start and end apart: 4, of which 3 were waited for; matrix products, arithmetic and copies ran while one was open for 11% of the time, Pallas kernels for 0%

profile of v1, /device:TPU:0, one launch (start us, length us, event | category | flops | bytes accessed | tf_op | source)
XLA Modules:
  0.0 367.1 jit_solution(5341161332522698862)
XLA Ops:
  7.2 0.0 copy-start
  7.2 0.0 all-gather.6.cloned.1.call-start
  7.2 1.3 dynamic-slice
  8.6 2.0 fusion.58
  10.6 2.0 broadcast_compare_fusion.1
  12.5 0.0 copy-start.4
  12.5 0.0 copy-start.5
  12.5 3.4 fusion.40
  15.9 0.0 copy-start.3
  15.9 0.0 all-gather.6.cloned.1.call-update
  16.0 0.0 all-gather.4.cloned.1.call-start
  16.0 0.7 all-gather.4.cloned.1.call-update
  16.7 0.0 copy-done.4
  16.7 0.1 fusion.52
  17.5 0.0 copy-done.5
  17.5 0.3 dynamic-update-slice.1
  17.8 10.1 %all-reduce.2 = (s32[4]{0:T(128)S(1)}, s32[1280]{0:T(1024)S(1)}) all-reduce(s32[4]{0:T(128)S(1)} %get-tuple-element.9, s32[1280]{0:T(1024)S(1)} %dynamic-update-slice.1), channel_id=1, replica_groups=mesh['grp'=2,'seq'=4,'head'=4] {'seq'}, use_global_device_ids=true, to_apply=%add | all-reduce | flops 1284 | bytes 10272
  27.9 0.6 compare_and_fusion
  28.6 36.0 %all-gather.6.cloned.1.call-done = bf16[64,128,128]{2,1,0:T(8,128)(2,1)} async-done(((bf16[16,128,128]{2,1,0:T(8,128)(2,1)}), bf16[64,128,128]{2,1,0:T(8,128)(2,1)}) %all-gather.6.cloned.1.call-update) | async-done | bytes 2097168 | tf_op jit(solution)/shard_map/all_gather | solution.py:47
  64.5 2.2 fusion.7
  66.8 0.0 copy-done.3
  66.8 2.7 fusion.35
  69.5 6.5 %multiply_reduce_fusion = (f32[320,16]{0,1:T(8,128)S(1)}, f32[320,16,128]{2,0,1:T(8,128)}) fusion(f32[16,128,320]{1,2,0:T(8,128)} %fusion.35, pred[320]{0:T(512)(128)(4,1)S(1)} %get-tuple-element.6, pred[320,320]{1,0:T(8,128)(4,1)S(1)} %fusion.52, bf16[320,2048]{1,0:T(8,128)(2,1)} %param.10, bf16[320,2048]{1,0:T(8,128)(2,1)} %param.9, ...), kind=kOutput, calls=%fused_computation.25 | convolution fusion | flops 844753920 | bytes 9298240 | tf_op jit(solution)/shard_map/hqk,khd->qhd/dot_general | solution.py:61
  75.9 2.7 fusion.13
  78.7 1.9 copy.35
  80.6 3.2 broadcast_in_dim_reshape.4
  83.8 0.2 collective-permute-start
  84.0 3.2 stack_broadcast_in_dim_reshape.3
  87.3 94.5 %collective-permute-done = bf16[1,320,2048]{2,1,0:T(8,128)(2,1)} collective-permute-done((bf16[1,320,2048]{2,1,0:T(8,128)(2,1)}, bf16[1,320,2048]{2,1,0:T(8,128)(2,1)}, u32[]{:S(2)}, u32[]{:S(2)}) %collective-permute-start) | collective-permute-done | bytes 1310752 | tf_op jit(solution)/shard_map/ppermute | solution.py:22
  181.8 2.0 pad_maximum_fusion.1
  183.7 3.5 fusion.16
  187.2 0.0 collective-permute-start.1
  187.2 0.0 copy-start.2
  187.2 0.4 fusion.21
  187.6 1.3 copy_bitcast_fusion.1
  188.9 113.3 %collective-permute-done.1 = bf16[2,320,2048]{2,1,0:T(8,128)(2,1)} collective-permute-done((bf16[2,320,2048]{2,1,0:T(8,128)(2,1)}, bf16[2,320,2048]{2,1,0:T(8,128)(2,1)}, u32[]{:S(2)}, u32[]{:S(2)}) %collective-permute-start.1) | collective-permute-done | bytes 2621472 | tf_op jit(solution)/shard_map/ppermute | solution.py:22
  302.1 0.0 copy-done.2
  302.1 2.2 pad_maximum_fusion
  304.4 1.8 reverse_select_fusion
  306.2 4.2 %copy.51 = bf16[160,8,16,128]{3,2,1,0:T(8,128)(2,1)} copy(bf16[160,8,16,128]{3,1,2,0:T(8,128)(2,1)S(1)} %bitcast.110) | data formatting | bytes 10485760
  310.3 7.9 %copy.38 = bf16[1280,2048]{0,1:T(8,128)(2,1)} copy(bf16[1280,2048]{1,0:T(8,128)(2,1)} %all-gather.4.cloned.1.call-done) | data formatting | bytes 10485760 | tf_op jit(solution)/shard_map/all_gather | solution.py:77
  318.2 0.0 copy-done
  318.2 12.9 %fusion = (f32[16,320]{1,0:T(8,128)S(1)}, f32[16,320,1280]{2,1,0:T(8,128)}) fusion(pred[320,1280]{1,0:T(8,128)(4,1)S(1)} %fusion.21, bf16[1280,16,128]{0,2,1:T(8,128)(2,1)} %bitcast.109, bf16[320,2048]{1,0:T(8,128)(2,1)S(1)} %copy-done), kind=kOutput, calls=%fused_computation.2 | convolution fusion | flops 1697377280 | bytes 33198080 | tf_op jit(solution)/shard_map/qhd,khd->hqk/dot_general | solution.py:84
  331.2 13.9 %fusion.1 = f32[16,320]{1,0:T(8,128)S(1)} fusion(f32[16,320,1280]{2,1,0:T(8,128)} %get-tuple-element.14, f32[16,320]{1,0:T(8,128)S(1)} %broadcast_maximum_fusion, pred[320,1280]{1,0:T(8,128)(4,1)S(1)} %fusion.21), kind=kLoop, calls=%fused_computation.3 | loop fusion | flops 32762880 | bytes 26664960 | tf_op jit(solution)/shard_map/reduce_sum | solution.py:95
  345.0 0.0 copy-start.1
  345.1 13.7 %fusion.22 = bf16[16,40,8,128]{3,2,1,0:T(8,128)(2,1)S(1)} fusion(bf16[1280,16,128]{2,1,0:T(8,128)(2,1)} %bitcast.111, f32[16,320,1280]{2,1,0:T(8,128)} %get-tuple-element.14, f32[16,320]{1,0:T(8,128)S(1)} %broadcast_maximum_fusion, pred[320,1280]{1,0:T(8,128)(4,1)S(1)} %fusion.21, f32[320,16]{0,1:T(8,128)S(1)} %bitcast.114), kind=kOutput, calls=%fused_computation.30 | convolution fusion | flops 1711800320 | bytes 33218560 | tf_op jit(solution)/shard_map/hqk,khd->qhd/dot_general | solution.py:96
  358.8 1.4 copy.99
  360.2 0.0 copy-done.1
  (7 shorter events, 0.0 us)
Async XLA Ops:
  7.2 311.1 %copy-start = (bf16[320,2048]{1,0:T(8,128)(2,1)S(1)}, bf16[320,2048]{1,0:T(8,128)(2,1)}, u32[]{:S(2)}) copy-start(bf16[320,2048]{1,0:T(8,128)(2,1)} %param.13) | copy-start | bytes 3932164
  7.2 57.4 %all-gather.6.cloned.1.call-start = ((), (), s32[]{:S(2)}) async-start(), calls=%async_computation.1 | async-start | bytes 2621440 | tf_op jit(solution)/shard_map/all_gather | solution.py:47
  12.5 4.2 %copy-start.4 = (s32[320]{0:T(512)S(1)}, s32[320]{0:T(512)}, u32[]{:S(2)}) copy-start(s32[320]{0:T(512)} %param.15) | copy-start | bytes 3844
  12.5 5.0 %copy-start.5 = (bf16[2048]{0:T(1024)(128)(2,1)S(1)}, bf16[2048]{0:T(1024)(128)(2,1)}, u32[]{:S(2)}) copy-start(bf16[2048]{0:T(1024)(128)(2,1)} %param.11) | copy-start | bytes 12292
  15.9 50.8 %copy-start.3 = (bf16[320,2048]{1,0:T(8,128)(2,1)S(1)}, bf16[320,2048]{1,0:T(8,128)(2,1)}, u32[]{:S(2)}) copy-start(bf16[320,2048]{1,0:T(8,128)(2,1)} %param.8) | copy-start | bytes 3932164
  16.0 294.4 %all-gather.4.cloned.1.call-start = ((), (), s32[]{:S(2)}) async-start(), calls=%async_computation | async-start | bytes 6553600 | tf_op jit(solution)/shard_map/all_gather | solution.py:77
  83.8 97.9 %collective-permute-start = (bf16[1,320,2048]{2,1,0:T(8,128)(2,1)}, bf16[1,320,2048]{2,1,0:T(8,128)(2,1)}, u32[]{:S(2)}, u32[]{:S(2)}) collective-permute-start(bf16[1,320,2048]{2,1,0:T(8,128)(2,1)} %broadcast_in_dim_reshape.4), channel_id=1, source_target_pairs={{0,4},{4,0},{8,12},{12,8},{1,5},{5,1},{9,13},{13,9},{2,6},{6,2},{1... | collective-permute-start | bytes 3932168 | tf_op jit(solution)/shard_map/ppermute | solution.py:22
  187.2 115.0 %collective-permute-start.1 = (bf16[2,320,2048]{2,1,0:T(8,128)(2,1)}, bf16[2,320,2048]{2,1,0:T(8,128)(2,1)}, u32[]{:S(2)}, u32[]{:S(2)}) collective-permute-start(bf16[2,320,2048]{2,1,0:T(8,128)(2,1)} %get-tuple-element.5), channel_id=1, source_target_pairs={{0,8},{4,12},{8,0},{12,4},{1,9},{5,13},{9,1},{13,5},{2,10},{6,14},... | collective-permute-start | bytes 7864328 | tf_op jit(solution)/shard_map/ppermute | solution.py:22
  187.2 114.9 %copy-start.2 = (bf16[1,2,320,2048]{3,2,1,0:T(8,128)(2,1)S(1)}, bf16[1,2,320,2048]{3,2,1,0:T(8,128)(2,1)}, u32[]{:S(2)}) copy-start(bf16[1,2,320,2048]{3,2,1,0:T(8,128)(2,1)} %get-tuple-element.4) | copy-start | bytes 7864324
  345.0 15.2 %copy-start.1 = (bf16[320,2048]{1,0:T(8,128)(2,1)S(1)}, bf16[320,2048]{1,0:T(8,128)(2,1)}, u32[]{:S(2)}) copy-start(bf16[320,2048]{1,0:T(8,128)(2,1)} %param.13) | copy-start | bytes 3932164
Sparse Core Ops, SparseCore 0:
  16.1 48.4 all-gather.5
  66.1 122.9 all-gather.3
